TPU v7x, 512 devices: a whole 4x4x16 slice. The times are simulated.
512 devices in a mesh: gx: 64 (over z, y), gy: 8 (over x, core).
Axes of the slice: x: 4, y: 4, z: 16, core: 2. Of those that a mesh axis runs over, the one named last changes fastest.
Arguments:
- rhs: float32 [64, 8, 128, 128], P('gx', 'gy'), may hold values from -57 to 57
- face_rows: int32 [64, 8, 4, 128], P('gx', 'gy'), may hold values from 0 to 127
- margin_weight: float32 [64, 8, 4, 128], P('gx', 'gy'), may hold values from 0.2 to 1
- local_blocks: bfloat16 [64, 8, 1, 128, 128], P('gx', 'gy'), may hold values from -0.4 to 4.4
- subdomain_inverse: bfloat16 [64, 8, 128, 640], P('gx', 'gy'), may hold values from -0.4 to 1.8
- coarse_basis: bfloat16 [64, 8, 128, 32], P('gx', 'gy'), may hold values from -0.5 to 0.5
- coarse_inverse: bfloat16 [64, 8, 32, 16384], P('gx', 'gy'), may hold values from -0.09765625 to 0.09765625
- coarse_map: int32 [512], replicated, may hold values from 0 to 511, each once
Outputs:
- solution: float32 [64, 8, 128, 128], P('gx', 'gy')
- relative_residual: float32 [128], replicated
Inputs may be any that keep to these rules, and one draw needn't show every extreme that they name: `face_rows`: rows of the subdomain, repeats possible. `coarse_map`: every position once.
All inputs are finite; a program needn't handle non-finite values.
Results may differ from a plain program's by a relative error of at most 0.004.
Values may be sent and summed in bfloat16 or wider, within the bound.
No kernel may reach another device: no remote copies, remote signals or barrier semaphores. Data moves between devices by JAX's collectives and lax.ppermute only.
A program may use at most 64 MiB of HBM per device.

v0:
```python
import jax
import numpy as np
import jax.numpy as jnp
from jax import lax
from jax.sharding import PartitionSpec as P

EPSILON = 1e-06
KEPT_SHARE = 1.0 / 64


def neighbours(rows, axis):
    count = lax.axis_size(axis)
    up = [(i, i + 1) for i in range(count - 1)]
    down = [(i + 1, i) for i in range(count - 1)]
    return (lax.ppermute(rows[1], axis, up), lax.ppermute(rows[0], axis, down))


def exchange(packs):
    below_first, above_first = neighbours(packs[0:2], "gx")
    below_second, above_second = neighbours(packs[2:4], "gy")
    return jnp.stack([below_first, above_first, below_second, above_second], axis=0)


def allsum(value):
    value = lax.psum(value, "gy")
    for axis in ("gx",):
        count = lax.axis_size(axis)
        if count & count - 1:
            value = lax.psum(value, axis)
            continue
        step = 1
        while step < count:
            value = value + lax.ppermute(value, axis, [(i, i ^ step) for i in range(count)])
            step *= 2
    return value


GATHER_ROUNDS = (("gx", 32), ("gx", 16), ("gx", 8), ("gx", 4), ("gx", 2), ("gx", 1))


def gather_rounds(count_x, count_y):
    sizes = {"gx": count_x, "gy": count_y}
    return tuple(((axis, step) for axis, step in GATHER_ROUNDS if step < sizes[axis]))


def doubling_gather(block, rounds):
    held = block[None]
    for axis, step in rounds:
        count = lax.axis_size(axis)
        got = lax.ppermute(held, axis, [(i, i ^ step) for i in range(count)])
        upper = lax.axis_index(axis) // step % 2 == 1
        held = jnp.where(
            upper, jnp.concatenate([got, held], axis=0), jnp.concatenate([held, got], axis=0)
        )
    return lax.all_gather(held.reshape(-1, block.shape[-1]), "gy", axis=0, tiled=True)


def gathered_order(rounds, count_y):
    order = []
    for outer in range(count_y):
        for position in range(2 ** len(rounds)):
            index = {"gx": 0, "gy": outer}
            for bit, (axis, step) in enumerate(rounds):
                index[axis] += (position >> bit & 1) * step
            order.append(index["gx"] * count_y + index["gy"])
    return np.asarray(order, np.int32)


def least_squares(scale_norm, first_dot, first_norm, cross_dot, second_dot, second_norm):
    radius_one = jnp.sqrt(first_dot * first_dot + first_norm * first_norm)
    cosine_one = first_dot / radius_one
    sine_one = first_norm / radius_one
    upper_entry = cosine_one * cross_dot + sine_one * second_dot
    lower_entry = cosine_one * second_dot - sine_one * cross_dot
    radius_two = jnp.sqrt(lower_entry * lower_entry + second_norm * second_norm)
    cosine_two = lower_entry / radius_two
    sine_two = second_norm / radius_two
    weight_two = -cosine_two * sine_one * scale_norm / radius_two
    weight_one = (cosine_one * scale_norm - upper_entry * weight_two) / radius_one
    return (weight_one, weight_two, sine_one * sine_two)


def on_device(
    rhs,
    face_rows,
    margin_weight,
    local_blocks,
    subdomain_inverse,
    coarse_basis,
    coarse_inverse,
    coarse_map,
):
    right_side = rhs[0, 0]
    margin_rows = face_rows[0, 0]
    margin_weights = margin_weight[0, 0]
    local_block = local_blocks[0, 0]
    inverse_rows = subdomain_inverse[0, 0]
    basis = coarse_basis[0, 0]
    coarse_rows = coarse_inverse[0, 0]
    owned_rows = right_side.shape[0]
    system_count = right_side.shape[1]
    basis_count = basis.shape[1]
    block_rows = local_block.shape[1]
    count_x = lax.axis_size("gx")
    count_y = lax.axis_size("gy")
    rounds = gather_rounds(count_x, count_y)
    gathered_map = coarse_map[gathered_order(rounds, count_y)]
    selection = (
        gathered_map[:, None] == jnp.arange(gathered_map.shape[0], dtype=jnp.int32)[None, :]
    ).astype(jnp.bfloat16)

    def margin_of(field):
        return exchange(field[margin_rows])

    def coarse_gather(residual):
        return doubling_gather(residual, rounds)

    def precondition(rounded, margin):
        extended = jnp.concatenate([rounded, margin.reshape(-1, system_count)], axis=0)
        local_part = jnp.dot(inverse_rows, extended, preferred_element_type=jnp.float32)
        residual = lax.dot_general(
            basis, rounded, (((0,), (0,)), ((), ())), preferred_element_type=jnp.float32
        ).astype(jnp.bfloat16)
        gathered = coarse_gather(residual).reshape(selection.shape[0], -1)
        placed = lax.dot_general(
            selection, gathered, (((0,), (0,)), ((), ())), preferred_element_type=jnp.float32
        ).astype(jnp.bfloat16)
        solved = jnp.dot(
            coarse_rows, placed.reshape(-1, system_count), preferred_element_type=jnp.float32
        )
        return local_part + jnp.dot(
            basis, solved.astype(jnp.bfloat16), preferred_element_type=jnp.float32
        )

    def apply_operator(vector):
        rounded = vector.astype(jnp.bfloat16)
        own_part = jnp.einsum(
            "brc,bcn->brn",
            local_block,
            rounded.reshape(-1, block_rows, system_count),
            preferred_element_type=jnp.float32,
        ).reshape(owned_rows, system_count)
        weighted = margin_weights[:, :, None] * margin_of(rounded).astype(jnp.float32)
        coupling = (
            jnp.zeros((owned_rows, system_count), jnp.float32)
            .at[margin_rows.reshape(-1)]
            .add(weighted.reshape(-1, system_count))
        )
        return own_part - coupling

    def column_norm(vector):
        return jnp.sqrt(allsum(jnp.sum(vector * vector, axis=0)) + EPSILON)

    def guarded_norm(expanded, whole, remainder):
        kept = jnp.all(jnp.isfinite(expanded) & (expanded >= KEPT_SHARE * whole))
        return lax.cond(kept, lambda vector: jnp.sqrt(expanded + EPSILON), column_norm, remainder)

    rhs_margin = margin_of(right_side)
    scale_norm = column_norm(right_side)
    krylov_one = right_side / scale_norm
    margin_one = rhs_margin / scale_norm
    precond_one = precondition(krylov_one.astype(jnp.bfloat16), margin_one.astype(jnp.bfloat16))
    applied = apply_operator(precond_one)
    applied_margin = margin_of(applied)
    sums = allsum(
        jnp.stack(
            [
                jnp.sum(applied * krylov_one, axis=0),
                jnp.sum(applied * applied, axis=0),
                jnp.sum(krylov_one * krylov_one, axis=0),
            ]
        )
    )
    first_dot = sums[0]
    remainder = applied - first_dot * krylov_one
    expanded = sums[1] - 2.0 * first_dot * first_dot + first_dot * first_dot * sums[2]
    first_norm = guarded_norm(expanded, sums[1], remainder)
    krylov_two = remainder / first_norm
    margin_two = (applied_margin - first_dot * margin_one) / first_norm
    precond_two = precondition(krylov_two.astype(jnp.bfloat16), margin_two.astype(jnp.bfloat16))
    applied = apply_operator(precond_two)
    dots = allsum(
        jnp.stack(
            [
                jnp.sum(applied * krylov_one, axis=0),
                jnp.sum(applied * krylov_two, axis=0),
                jnp.sum(applied * applied, axis=0),
                jnp.sum(krylov_one * krylov_one, axis=0),
                jnp.sum(krylov_one * krylov_two, axis=0),
                jnp.sum(krylov_two * krylov_two, axis=0),
            ]
        )
    )
    cross_dot = dots[0]
    second_dot = dots[1]
    remainder = applied - cross_dot * krylov_one - second_dot * krylov_two
    expanded = (
        dots[2]
        - 2.0 * cross_dot * cross_dot
        - 2.0 * second_dot * second_dot
        + cross_dot * cross_dot * dots[3]
        + 2.0 * cross_dot * second_dot * dots[4]
        + second_dot * second_dot * dots[5]
    )
    second_norm = guarded_norm(expanded, dots[2], remainder)
    weight_one, weight_two, relative = least_squares(
        scale_norm, first_dot, first_norm, cross_dot, second_dot, second_norm
    )
    solution = weight_one * precond_one + weight_two * precond_two
    return (solution[None, None], relative)


def solution(mesh):
    return jax.shard_map(
        on_device,
        mesh=mesh,
        in_specs=(
            P("gx", "gy", None, None),
            P("gx", "gy", None, None),
            P("gx", "gy", None, None),
            P("gx", "gy", None, None, None),
            P("gx", "gy", None, None),
            P("gx", "gy", None, None),
            P("gx", "gy", None, None),
            P(),
        ),
        out_specs=(P("gx", "gy", None, None), P()),
        check_vma=False,
    )
```

profile of v0, /device:TPU:8, one launch (start us, length us, event | category | flops | bytes accessed | tf_op | source)
XLA Modules:
  0.0 481.7 jit_solution(6558370175424277475)
XLA Ops:
  8.2 14.6 %psum.35 = f32[128]{0:T(128)S(1)} all-reduce(f32[128]{0:T(128)S(1)} %multiply_reduce_fusion.10), channel_id=1, replica_groups=mesh['gx'=64,'gy'=8] {'gy'}, use_global_device_ids=true, to_apply=%region_1.0 | all-reduce | flops 128 | bytes 1024 | tf_op jit(solution)/shard_map/psum | solution.py:25
  22.8 5.5 %collective-permute-start.12 = (f32[128]{0:T(128)S(1)}, f32[128]{0:T(128)S(1)}, u32[]{:S(2)}, u32[]{:S(2)}) collective-permute-start(f32[128]{0:T(128)S(1)} %psum.35), channel_id=1, source_target_pairs={{0,8},{8,0},{16,24},{24,16},{32,40},{40,32},{48,56},{56,48},{64,72... | collective-permute-start | bytes 1544 | tf_op jit(solution)/shard_map/ppermute | solution.py:33
  32.5 4.3 collective-permute-done.13
  48.6 7.9 %collective-permute-start.16 = (f32[128]{0:T(128)S(1)}, f32[128]{0:T(128)S(1)}, u32[]{:S(2)}, u32[]{:S(2)}) collective-permute-start(f32[128]{0:T(128)S(1)} %add.222), channel_id=1, source_target_pairs={{0,128},{8,136},{16,144},{24,152},{32,160},{40,168},{48,176},{56,1... | collective-permute-start | bytes 1544 | tf_op jit(solution)/shard_map/ppermute | solution.py:33
  58.0 14.1 %collective-permute-start.17 = (f32[128]{0:T(128)S(1)}, f32[128]{0:T(128)S(1)}, u32[]{:S(2)}, u32[]{:S(2)}) collective-permute-start(f32[128]{0:T(128)S(1)} %add.223), channel_id=1, source_target_pairs={{0,256},{8,264},{16,272},{24,280},{32,288},{40,296},{48,304},{56,3... | collective-permute-start | bytes 1544 | tf_op jit(solution)/shard_map/ppermute | solution.py:33
  74.6 12.6 %collective-permute-start.22 = (bf16[1,32,128]{2,1,0:T(8,128)(2,1)S(1)}, bf16[1,32,128]{2,1,0:T(8,128)(2,1)S(1)}, u32[]{:S(2)}, u32[]{:S(2)}) collective-permute-start(bf16[1,32,128]{2,1,0:T(8,128)(2,1)S(1)} %fusion.2), channel_id=1, source_target_pairs={{0,256},{8,264},{16,272},{24,280},{32,288},{40,296},{48,304},{56,3... | collective-permute-start | bytes 24584 | tf_op jit(solution)/shard_map/ppermute | solution.py:50
  88.9 6.4 %collective-permute-start.23 = (bf16[2,32,128]{2,1,0:T(8,128)(2,1)S(1)}, bf16[2,32,128]{2,1,0:T(8,128)(2,1)S(1)}, u32[]{:S(2)}, u32[]{:S(2)}) collective-permute-start(bf16[2,32,128]{2,1,0:T(8,128)(2,1)S(1)} %maximum_select_fusion.10), channel_id=1, source_target_pairs={{0,128},{8,136},{16,144},{24,152},{32,160},{40,168},{48,176},{56,1... | collective-permute-start | bytes 49160 | tf_op jit(solution)/shard_map/ppermute | solution.py:50
  111.4 4.3 collective-permute-start.26
  115.7 4.1 collective-permute-done.26
  122.3 5.8 %collective-permute-done.27 = bf16[32,32,128]{2,1,0:T(8,128)(2,1)S(1)} collective-permute-done((bf16[32,32,128]{2,1,0:T(8,128)(2,1)S(1)}, bf16[32,32,128]{2,1,0:T(8,128)(2,1)S(1)}, u32[]{:S(2)}, u32[]{:S(2)}) %collective-permute-start.27) | collective-permute-done | bytes 262176 | tf_op jit(solution)/shard_map/ppermute | solution.py:50
  143.3 24.8 %all-gather.3.cloned.1.call-done = bf16[16384,128]{1,0:T(8,128)(2,1)} async-done(((bf16[2048,128]{1,0:T(8,128)(2,1)}), bf16[16384,128]{1,0:T(8,128)(2,1)}) %all-gather.3.cloned.1.call-update) | async-done | bytes 4194320 | tf_op jit(solution)/shard_map/all_gather | solution.py:55
  168.1 7.4 %reshape.132 = bf16[512,4096]{1,0:T(8,128)(2,1)} reshape(bf16[16384,128]{1,0:T(8,128)(2,1)} %all-gather.3.cloned.1.call-done) | data formatting | bytes 8388608 | tf_op jit(solution)/shard_map/reshape | solution.py:124
  175.4 6.6 %convolution_convert_fusion.1 = bf16[512,4096]{1,0:T(8,128)(2,1)} fusion(bf16[512,4096]{1,0:T(8,128)(2,1)} %reshape.132, s32[512]{0:T(512)S(1)} %gather_fusion.1), kind=kOutput, calls=%fused_computation.10 | convolution fusion | flops 2149842944 | bytes 8390656 | tf_op jit(solution)/shard_map/dot_general | solution.py:125
  182.0 7.5 %reshape.133 = bf16[16384,128]{1,0:T(8,128)(2,1)} reshape(bf16[512,4096]{1,0:T(8,128)(2,1)} %convolution_convert_fusion.1) | data formatting | bytes 8388608 | tf_op jit(solution)/shard_map/reshape | solution.py:129
  208.4 14.6 %psum.36 = f32[3,128]{1,0:T(4,128)S(1)} all-reduce(f32[3,128]{1,0:T(4,128)S(1)} %pad_maximum_fusion.4), channel_id=1, replica_groups=mesh['gx'=64,'gy'=8] {'gy'}, use_global_device_ids=true, to_apply=%region_6.7 | all-reduce | flops 384 | bytes 3072 | tf_op jit(solution)/shard_map/psum | solution.py:25
  235.4 4.1 collective-permute-start.34
  241.1 4.9 %collective-permute-start.35 = (f32[3,128]{1,0:T(4,128)S(1)}, f32[3,128]{1,0:T(4,128)S(1)}, u32[]{:S(2)}, u32[]{:S(2)}) collective-permute-start(f32[3,128]{1,0:T(4,128)S(1)} %add.239), channel_id=1, source_target_pairs={{0,64},{8,72},{16,80},{24,88},{32,96},{40,104},{48,112},{56,120},{... | collective-permute-start | bytes 4616 | tf_op jit(solution)/shard_map/ppermute | solution.py:33
  247.6 9.2 %collective-permute-start.36 = (f32[3,128]{1,0:T(4,128)S(1)}, f32[3,128]{1,0:T(4,128)S(1)}, u32[]{:S(2)}, u32[]{:S(2)}) collective-permute-start(f32[3,128]{1,0:T(4,128)S(1)} %add.240), channel_id=1, source_target_pairs={{0,128},{8,136},{16,144},{24,152},{32,160},{40,168},{48,176},{56,1... | collective-permute-start | bytes 4616 | tf_op jit(solution)/shard_map/ppermute | solution.py:33
  258.3 13.0 %collective-permute-start.37 = (f32[3,128]{1,0:T(4,128)S(1)}, f32[3,128]{1,0:T(4,128)S(1)}, u32[]{:S(2)}, u32[]{:S(2)}) collective-permute-start(f32[3,128]{1,0:T(4,128)S(1)} %add.241), channel_id=1, source_target_pairs={{0,256},{8,264},{16,272},{24,280},{32,288},{40,296},{48,304},{56,3... | collective-permute-start | bytes 4616 | tf_op jit(solution)/shard_map/ppermute | solution.py:33
  274.4 12.6 %collective-permute-start.42 = (bf16[1,32,128]{2,1,0:T(8,128)(2,1)S(1)}, bf16[1,32,128]{2,1,0:T(8,128)(2,1)S(1)}, u32[]{:S(2)}, u32[]{:S(2)}) collective-permute-start(bf16[1,32,128]{2,1,0:T(8,128)(2,1)S(1)} %fusion.3), channel_id=1, source_target_pairs={{0,256},{8,264},{16,272},{24,280},{32,288},{40,296},{48,304},{56,3... | collective-permute-start | bytes 24584 | tf_op jit(solution)/shard_map/ppermute | solution.py:50
  288.6 7.5 %collective-permute-start.43 = (bf16[2,32,128]{2,1,0:T(8,128)(2,1)S(1)}, bf16[2,32,128]{2,1,0:T(8,128)(2,1)S(1)}, u32[]{:S(2)}, u32[]{:S(2)}) collective-permute-start(bf16[2,32,128]{2,1,0:T(8,128)(2,1)S(1)} %maximum_select_fusion.11), channel_id=1, source_target_pairs={{0,128},{8,136},{16,144},{24,152},{32,160},{40,168},{48,176},{56,1... | collective-permute-start | bytes 49160 | tf_op jit(solution)/shard_map/ppermute | solution.py:50
  314.7 4.7 collective-permute-done.46
  323.4 4.3 collective-permute-done.47
  340.4 26.8 %all-gather.5.cloned.1.call-done = bf16[16384,128]{1,0:T(8,128)(2,1)} async-done(((bf16[2048,128]{1,0:T(8,128)(2,1)}), bf16[16384,128]{1,0:T(8,128)(2,1)}) %all-gather.5.cloned.1.call-update) | async-done | bytes 4194320 | tf_op jit(solution)/shard_map/all_gather | solution.py:55
  367.2 7.4 %reshape.135 = bf16[512,4096]{1,0:T(8,128)(2,1)} reshape(bf16[16384,128]{1,0:T(8,128)(2,1)} %all-gather.5.cloned.1.call-done) | data formatting | bytes 8388608 | tf_op jit(solution)/shard_map/reshape | solution.py:124
  374.6 6.6 %convolution_convert_fusion = bf16[512,4096]{1,0:T(8,128)(2,1)} fusion(bf16[512,4096]{1,0:T(8,128)(2,1)} %reshape.135, s32[512]{0:T(512)S(1)} %gather_fusion.1), kind=kOutput, calls=%fused_computation.9 | convolution fusion | flops 2149842944 | bytes 8390656 | tf_op jit(solution)/shard_map/dot_general | solution.py:125
  381.2 7.4 %reshape.136 = bf16[16384,128]{1,0:T(8,128)(2,1)} reshape(bf16[512,4096]{1,0:T(8,128)(2,1)} %convolution_convert_fusion) | data formatting | bytes 8388608 | tf_op jit(solution)/shard_map/reshape | solution.py:129
  407.4 14.6 %psum.37 = f32[6,128]{1,0:T(8,128)S(1)} all-reduce(f32[6,128]{1,0:T(8,128)S(1)} %stack.126), channel_id=1, replica_groups=mesh['gx'=64,'gy'=8] {'gy'}, use_global_device_ids=true, to_apply=%region_18.19 | all-reduce | flops 768 | bytes 6144 | tf_op jit(solution)/shard_map/psum | solution.py:25
  434.6 4.1 collective-permute-start.54
  440.2 4.9 %collective-permute-start.55 = (f32[6,128]{1,0:T(8,128)S(1)}, f32[6,128]{1,0:T(8,128)S(1)}, u32[]{:S(2)}, u32[]{:S(2)}) collective-permute-start(f32[6,128]{1,0:T(8,128)S(1)} %add.249), channel_id=1, source_target_pairs={{0,64},{8,72},{16,80},{24,88},{32,96},{40,104},{48,112},{56,120},{... | collective-permute-start | bytes 9224 | tf_op jit(solution)/shard_map/ppermute | solution.py:33
  446.7 9.2 %collective-permute-start.56 = (f32[6,128]{1,0:T(8,128)S(1)}, f32[6,128]{1,0:T(8,128)S(1)}, u32[]{:S(2)}, u32[]{:S(2)}) collective-permute-start(f32[6,128]{1,0:T(8,128)S(1)} %add.250), channel_id=1, source_target_pairs={{0,128},{8,136},{16,144},{24,152},{32,160},{40,168},{48,176},{56,1... | collective-permute-start | bytes 9224 | tf_op jit(solution)/shard_map/ppermute | solution.py:33
  457.5 13.0 %collective-permute-start.57 = (f32[6,128]{1,0:T(8,128)S(1)}, f32[6,128]{1,0:T(8,128)S(1)}, u32[]{:S(2)}, u32[]{:S(2)}) collective-permute-start(f32[6,128]{1,0:T(8,128)S(1)} %add.251), channel_id=1, source_target_pairs={{0,256},{8,264},{16,272},{24,280},{32,288},{40,296},{48,304},{56,3... | collective-permute-start | bytes 9224 | tf_op jit(solution)/shard_map/ppermute | solution.py:33
  (173 shorter events, 170.4 us)
Async XLA Ops:
  7.2 160.9 %all-gather.3.cloned.1.call-start = ((), (), s32[]{:S(2)}) async-start(), calls=%async_computation | async-start | bytes 4718592 | tf_op jit(solution)/shard_map/all_gather | solution.py:55
  22.8 7.0 %collective-permute-start.12 = (f32[128]{0:T(128)S(1)}, f32[128]{0:T(128)S(1)}, u32[]{:S(2)}, u32[]{:S(2)}) collective-permute-start(f32[128]{0:T(128)S(1)} %psum.35), channel_id=1, source_target_pairs={{0,8},{8,0},{16,24},{24,16},{32,40},{40,32},{48,56},{56,48},{64,72... | collective-permute-start | bytes 1544 | tf_op jit(solution)/shard_map/ppermute | solution.py:33
  29.9 7.0 %collective-permute-start.13 = (f32[128]{0:T(128)S(1)}, f32[128]{0:T(128)S(1)}, u32[]{:S(2)}, u32[]{:S(2)}) collective-permute-start(f32[128]{0:T(128)S(1)} %add.219), channel_id=1, source_target_pairs={{0,16},{8,24},{16,0},{24,8},{32,48},{40,56},{48,32},{56,40},{64,80... | collective-permute-start | bytes 1544 | tf_op jit(solution)/shard_map/ppermute | solution.py:33
  42.3 6.3 %collective-permute-start.15 = (f32[128]{0:T(128)S(1)}, f32[128]{0:T(128)S(1)}, u32[]{:S(2)}, u32[]{:S(2)}) collective-permute-start(f32[128]{0:T(128)S(1)} %add.221), channel_id=1, source_target_pairs={{0,64},{8,72},{16,80},{24,88},{32,96},{40,104},{48,112},{56,120},{... | collective-permute-start | bytes 1544 | tf_op jit(solution)/shard_map/ppermute | solution.py:33
  48.6 9.4 %collective-permute-start.16 = (f32[128]{0:T(128)S(1)}, f32[128]{0:T(128)S(1)}, u32[]{:S(2)}, u32[]{:S(2)}) collective-permute-start(f32[128]{0:T(128)S(1)} %add.222), channel_id=1, source_target_pairs={{0,128},{8,136},{16,144},{24,152},{32,160},{40,168},{48,176},{56,1... | collective-permute-start | bytes 1544 | tf_op jit(solution)/shard_map/ppermute | solution.py:33
  58.0 15.6 %collective-permute-start.17 = (f32[128]{0:T(128)S(1)}, f32[128]{0:T(128)S(1)}, u32[]{:S(2)}, u32[]{:S(2)}) collective-permute-start(f32[128]{0:T(128)S(1)} %add.223), channel_id=1, source_target_pairs={{0,256},{8,264},{16,272},{24,280},{32,288},{40,296},{48,304},{56,3... | collective-permute-start | bytes 1544 | tf_op jit(solution)/shard_map/ppermute | solution.py:33
  74.6 14.3 %collective-permute-start.22 = (bf16[1,32,128]{2,1,0:T(8,128)(2,1)S(1)}, bf16[1,32,128]{2,1,0:T(8,128)(2,1)S(1)}, u32[]{:S(2)}, u32[]{:S(2)}) collective-permute-start(bf16[1,32,128]{2,1,0:T(8,128)(2,1)S(1)} %fusion.2), channel_id=1, source_target_pairs={{0,256},{8,264},{16,272},{24,280},{32,288},{40,296},{48,304},{56,3... | collective-permute-start | bytes 24584 | tf_op jit(solution)/shard_map/ppermute | solution.py:50
  88.9 9.5 %collective-permute-start.23 = (bf16[2,32,128]{2,1,0:T(8,128)(2,1)S(1)}, bf16[2,32,128]{2,1,0:T(8,128)(2,1)S(1)}, u32[]{:S(2)}, u32[]{:S(2)}) collective-permute-start(bf16[2,32,128]{2,1,0:T(8,128)(2,1)S(1)} %maximum_select_fusion.10), channel_id=1, source_target_pairs={{0,128},{8,136},{16,144},{24,152},{32,160},{40,168},{48,176},{56,1... | collective-permute-start | bytes 49160 | tf_op jit(solution)/shard_map/ppermute | solution.py:50
  98.5 6.7 %collective-permute-start.24 = (bf16[4,32,128]{2,1,0:T(8,128)(2,1)S(1)}, bf16[4,32,128]{2,1,0:T(8,128)(2,1)S(1)}, u32[]{:S(2)}, u32[]{:S(2)}) collective-permute-start(bf16[4,32,128]{2,1,0:T(8,128)(2,1)S(1)} %maximum_select_fusion.8), channel_id=1, source_target_pairs={{0,64},{8,72},{16,80},{24,88},{32,96},{40,104},{48,112},{56,120},{... | collective-permute-start | bytes 98312 | tf_op jit(solution)/shard_map/ppermute | solution.py:50
  111.4 8.5 %collective-permute-start.26 = (bf16[16,32,128]{2,1,0:T(8,128)(2,1)S(1)}, bf16[16,32,128]{2,1,0:T(8,128)(2,1)S(1)}, u32[]{:S(2)}, u32[]{:S(2)}) collective-permute-start(bf16[16,32,128]{2,1,0:T(8,128)(2,1)S(1)} %maximum_select_fusion.4), channel_id=1, source_target_pairs={{0,16},{8,24},{16,0},{24,8},{32,48},{40,56},{48,32},{56,40},{64,80... | collective-permute-start | bytes 393224 | tf_op jit(solution)/shard_map/ppermute | solution.py:50
  119.9 8.3 %collective-permute-start.27 = (bf16[32,32,128]{2,1,0:T(8,128)(2,1)S(1)}, bf16[32,32,128]{2,1,0:T(8,128)(2,1)S(1)}, u32[]{:S(2)}, u32[]{:S(2)}) collective-permute-start(bf16[32,32,128]{2,1,0:T(8,128)(2,1)S(1)} %maximum_select_fusion.2), channel_id=1, source_target_pairs={{0,8},{8,0},{16,24},{24,16},{32,40},{40,32},{48,56},{56,48},{64,72... | collective-permute-start | bytes 786440 | tf_op jit(solution)/shard_map/ppermute | solution.py:50
  129.1 238.1 %all-gather.5.cloned.1.call-start = ((), (), s32[]{:S(2)}) async-start(), calls=%async_computation.1 | async-start | bytes 4718592 | tf_op jit(solution)/shard_map/all_gather | solution.py:55
  130.9 12.0 %collective-permute-start.18 = (f32[128,128]{1,0:T(8,128)S(1)}, f32[128,128]{1,0:T(8,128)S(1)}, u32[]{:S(2)}, u32[]{:S(2)}) collective-permute-start(f32[128,128]{1,0:T(8,128)S(1)} %get-tuple-element.64), channel_id=1, source_target_pairs={{0,8},{8,16},{16,24},{24,32},{32,40},{40,48},{48,56},{56,64},{64,7... | collective-permute-start | bytes 196616 | tf_op jit(solution)/shard_map/ppermute | solution.py:15
  134.4 8.5 %collective-permute-start.20 = (f32[128,128]{1,0:T(8,128)S(1)}, f32[128,128]{1,0:T(8,128)S(1)}, u32[]{:S(2)}, u32[]{:S(2)}) collective-permute-start(f32[128,128]{1,0:T(8,128)S(1)} %get-tuple-element.65), channel_id=1, source_target_pairs={{0,1},{1,2},{2,3},{3,4},{4,5},{5,6},{6,7},{8,9},{9,10},{10,11},{11... | collective-permute-start | bytes 196616 | tf_op jit(solution)/shard_map/ppermute | solution.py:15
  135.7 7.2 %collective-permute-start.19 = (f32[128,128]{1,0:T(8,128)S(1)}, f32[128,128]{1,0:T(8,128)S(1)}, u32[]{:S(2)}, u32[]{:S(2)}) collective-permute-start(f32[128,128]{1,0:T(8,128)S(1)} %get-tuple-element.66), channel_id=1, source_target_pairs={{8,0},{16,8},{24,16},{32,24},{40,32},{48,40},{56,48},{64,56},{72,6... | collective-permute-start | bytes 196616 | tf_op jit(solution)/shard_map/ppermute | solution.py:15
  194.6 9.1 %collective-permute-start.28 = (bf16[128,128]{1,0:T(8,128)(2,1)S(1)}, bf16[128,128]{1,0:T(8,128)(2,1)S(1)}, u32[]{:S(2)}, u32[]{:S(2)}) collective-permute-start(bf16[128,128]{1,0:T(8,128)(2,1)S(1)} %get-tuple-element.72), channel_id=1, source_target_pairs={{0,8},{8,16},{16,24},{24,32},{32,40},{40,48},{48,56},{56,64},{64,7... | collective-permute-start | bytes 98312 | tf_op jit(solution)/shard_map/ppermute | solution.py:15
  228.5 7.0 %collective-permute-start.33 = (f32[3,128]{1,0:T(4,128)S(1)}, f32[3,128]{1,0:T(4,128)S(1)}, u32[]{:S(2)}, u32[]{:S(2)}) collective-permute-start(f32[3,128]{1,0:T(4,128)S(1)} %add.237), channel_id=1, source_target_pairs={{0,16},{8,24},{16,0},{24,8},{32,48},{40,56},{48,32},{56,40},{64,80... | collective-permute-start | bytes 4616 | tf_op jit(solution)/shard_map/ppermute | solution.py:33
  241.1 6.5 %collective-permute-start.35 = (f32[3,128]{1,0:T(4,128)S(1)}, f32[3,128]{1,0:T(4,128)S(1)}, u32[]{:S(2)}, u32[]{:S(2)}) collective-permute-start(f32[3,128]{1,0:T(4,128)S(1)} %add.239), channel_id=1, source_target_pairs={{0,64},{8,72},{16,80},{24,88},{32,96},{40,104},{48,112},{56,120},{... | collective-permute-start | bytes 4616 | tf_op jit(solution)/shard_map/ppermute | solution.py:33
  247.6 10.8 %collective-permute-start.36 = (f32[3,128]{1,0:T(4,128)S(1)}, f32[3,128]{1,0:T(4,128)S(1)}, u32[]{:S(2)}, u32[]{:S(2)}) collective-permute-start(f32[3,128]{1,0:T(4,128)S(1)} %add.240), channel_id=1, source_target_pairs={{0,128},{8,136},{16,144},{24,152},{32,160},{40,168},{48,176},{56,1... | collective-permute-start | bytes 4616 | tf_op jit(solution)/shard_map/ppermute | solution.py:33
  258.3 14.5 %collective-permute-start.37 = (f32[3,128]{1,0:T(4,128)S(1)}, f32[3,128]{1,0:T(4,128)S(1)}, u32[]{:S(2)}, u32[]{:S(2)}) collective-permute-start(f32[3,128]{1,0:T(4,128)S(1)} %add.241), channel_id=1, source_target_pairs={{0,256},{8,264},{16,272},{24,280},{32,288},{40,296},{48,304},{56,3... | collective-permute-start | bytes 4616 | tf_op jit(solution)/shard_map/ppermute | solution.py:33
  274.4 14.3 %collective-permute-start.42 = (bf16[1,32,128]{2,1,0:T(8,128)(2,1)S(1)}, bf16[1,32,128]{2,1,0:T(8,128)(2,1)S(1)}, u32[]{:S(2)}, u32[]{:S(2)}) collective-permute-start(bf16[1,32,128]{2,1,0:T(8,128)(2,1)S(1)} %fusion.3), channel_id=1, source_target_pairs={{0,256},{8,264},{16,272},{24,280},{32,288},{40,296},{48,304},{56,3... | collective-permute-start | bytes 24584 | tf_op jit(solution)/shard_map/ppermute | solution.py:50
  288.6 9.5 %collective-permute-start.43 = (bf16[2,32,128]{2,1,0:T(8,128)(2,1)S(1)}, bf16[2,32,128]{2,1,0:T(8,128)(2,1)S(1)}, u32[]{:S(2)}, u32[]{:S(2)}) collective-permute-start(bf16[2,32,128]{2,1,0:T(8,128)(2,1)S(1)} %maximum_select_fusion.11), channel_id=1, source_target_pairs={{0,128},{8,136},{16,144},{24,152},{32,160},{40,168},{48,176},{56,1... | collective-permute-start | bytes 49160 | tf_op jit(solution)/shard_map/ppermute | solution.py:50
  298.2 6.7 %collective-permute-start.44 = (bf16[4,32,128]{2,1,0:T(8,128)(2,1)S(1)}, bf16[4,32,128]{2,1,0:T(8,128)(2,1)S(1)}, u32[]{:S(2)}, u32[]{:S(2)}) collective-permute-start(bf16[4,32,128]{2,1,0:T(8,128)(2,1)S(1)} %maximum_select_fusion.9), channel_id=1, source_target_pairs={{0,64},{8,72},{16,80},{24,88},{32,96},{40,104},{48,112},{56,120},{... | collective-permute-start | bytes 98312 | tf_op jit(solution)/shard_map/ppermute | solution.py:50
  311.1 8.4 %collective-permute-start.46 = (bf16[16,32,128]{2,1,0:T(8,128)(2,1)S(1)}, bf16[16,32,128]{2,1,0:T(8,128)(2,1)S(1)}, u32[]{:S(2)}, u32[]{:S(2)}) collective-permute-start(bf16[16,32,128]{2,1,0:T(8,128)(2,1)S(1)} %maximum_select_fusion.5), channel_id=1, source_target_pairs={{0,16},{8,24},{16,0},{24,8},{32,48},{40,56},{48,32},{56,40},{64,80... | collective-permute-start | bytes 393224 | tf_op jit(solution)/shard_map/ppermute | solution.py:50
  319.5 8.3 %collective-permute-start.47 = (bf16[32,32,128]{2,1,0:T(8,128)(2,1)S(1)}, bf16[32,32,128]{2,1,0:T(8,128)(2,1)S(1)}, u32[]{:S(2)}, u32[]{:S(2)}) collective-permute-start(bf16[32,32,128]{2,1,0:T(8,128)(2,1)S(1)} %maximum_select_fusion.3), channel_id=1, source_target_pairs={{0,8},{8,0},{16,24},{24,16},{32,40},{40,32},{48,56},{56,48},{64,72... | collective-permute-start | bytes 786440 | tf_op jit(solution)/shard_map/ppermute | solution.py:50
  329.7 8.6 %collective-permute-start.38 = (f32[128,128]{1,0:T(8,128)S(1)}, f32[128,128]{1,0:T(8,128)S(1)}, u32[]{:S(2)}, u32[]{:S(2)}) collective-permute-start(f32[128,128]{1,0:T(8,128)S(1)} %get-tuple-element.60), channel_id=1, source_target_pairs={{0,8},{8,16},{16,24},{24,32},{32,40},{40,48},{48,56},{56,64},{64,7... | collective-permute-start | bytes 196616 | tf_op jit(solution)/shard_map/ppermute | solution.py:15
  331.9 6.5 %collective-permute-start.40 = (f32[128,128]{1,0:T(8,128)S(1)}, f32[128,128]{1,0:T(8,128)S(1)}, u32[]{:S(2)}, u32[]{:S(2)}) collective-permute-start(f32[128,128]{1,0:T(8,128)S(1)} %get-tuple-element.61), channel_id=1, source_target_pairs={{0,1},{1,2},{2,3},{3,4},{4,5},{5,6},{6,7},{8,9},{9,10},{10,11},{11... | collective-permute-start | bytes 196616 | tf_op jit(solution)/shard_map/ppermute | solution.py:15
  393.7 9.0 %collective-permute-start.48 = (bf16[128,128]{1,0:T(8,128)(2,1)S(1)}, bf16[128,128]{1,0:T(8,128)(2,1)S(1)}, u32[]{:S(2)}, u32[]{:S(2)}) collective-permute-start(bf16[128,128]{1,0:T(8,128)(2,1)S(1)} %get-tuple-element.68), channel_id=1, source_target_pairs={{0,8},{8,16},{16,24},{24,32},{32,40},{40,48},{48,56},{56,64},{64,7... | collective-permute-start | bytes 98312 | tf_op jit(solution)/shard_map/ppermute | solution.py:15
  427.6 7.0 %collective-permute-start.53 = (f32[6,128]{1,0:T(8,128)S(1)}, f32[6,128]{1,0:T(8,128)S(1)}, u32[]{:S(2)}, u32[]{:S(2)}) collective-permute-start(f32[6,128]{1,0:T(8,128)S(1)} %add.247), channel_id=1, source_target_pairs={{0,16},{8,24},{16,0},{24,8},{32,48},{40,56},{48,32},{56,40},{64,80... | collective-permute-start | bytes 9224 | tf_op jit(solution)/shard_map/ppermute | solution.py:33
  440.2 6.5 %collective-permute-start.55 = (f32[6,128]{1,0:T(8,128)S(1)}, f32[6,128]{1,0:T(8,128)S(1)}, u32[]{:S(2)}, u32[]{:S(2)}) collective-permute-start(f32[6,128]{1,0:T(8,128)S(1)} %add.249), channel_id=1, source_target_pairs={{0,64},{8,72},{16,80},{24,88},{32,96},{40,104},{48,112},{56,120},{... | collective-permute-start | bytes 9224 | tf_op jit(solution)/shard_map/ppermute | solution.py:33
  446.7 10.8 %collective-permute-start.56 = (f32[6,128]{1,0:T(8,128)S(1)}, f32[6,128]{1,0:T(8,128)S(1)}, u32[]{:S(2)}, u32[]{:S(2)}) collective-permute-start(f32[6,128]{1,0:T(8,128)S(1)} %add.250), channel_id=1, source_target_pairs={{0,128},{8,136},{16,144},{24,152},{32,160},{40,168},{48,176},{56,1... | collective-permute-start | bytes 9224 | tf_op jit(solution)/shard_map/ppermute | solution.py:33
  457.5 14.6 %collective-permute-start.57 = (f32[6,128]{1,0:T(8,128)S(1)}, f32[6,128]{1,0:T(8,128)S(1)}, u32[]{:S(2)}, u32[]{:S(2)}) collective-permute-start(f32[6,128]{1,0:T(8,128)S(1)} %add.251), channel_id=1, source_target_pairs={{0,256},{8,264},{16,272},{24,280},{32,288},{40,296},{48,304},{56,3... | collective-permute-start | bytes 9224 | tf_op jit(solution)/shard_map/ppermute | solution.py:33
  (25 other events, 741.4 us)
Sparse Core Ops, SparseCore 0:
  129.2 38.8 all-gather.2
  328.8 38.3 all-gather.4
where the time goes:
time: 484 us; the launch traced here: 482 us
  starting transfers between devices  210 us (43%)
  waiting for transfers between devices  139 us (29%)
  blocking collectives  43.9 us (9%)
  local copies, waits for them, and re-layouts  39 us (8%)
  matrix products  22.4 us (5%)
  between operations  16.4 us (3%)
  other arithmetic  10.6 us (2%)
    ppermute x18, starting transfers between devices, allsum(): lax.ppermute(value, axis, [(i, i ^ step) for i in range(count)])  110 us
    ppermute x12, starting transfers between devices, doubling_gather(): got = lax.ppermute(held, axis, [(i, i ^ step) for i in range(count)])  65.1 us
    all_gather x2, waiting for transfers between devices, doubling_gather(): lax.all_gather(held.reshape(-1, block.shape[-1]), 'gy', axis=0, tiled=True)  51.6 us
    psum x3, blocking collectives, allsum(): value = lax.psum(value, 'gy')  43.9 us
    ppermute x12, waiting for transfers between devices, doubling_gather(): got = lax.ppermute(held, axis, [(i, i ^ step) for i in range(count)])  41.3 us
    ppermute x18, waiting for transfers between devices, allsum(): lax.ppermute(value, axis, [(i, i ^ step) for i in range(count)])  40.5 us
    ppermute x16, starting transfers between devices, neighbours(): return (lax.ppermute(rows[1], axis, up), lax.ppermute(rows[0], axis, down))  35 us
    reshape x2, local copies, waits for them, and re-layouts, precondition(): placed.reshape(-1, system_count)  14.9 us
  transfers between devices with their start and end apart: 48, of which 36 were waited for; matrix products, arithmetic and copies ran while one was open for 1% of the time, Pallas kernels for 0%

commit v1 on v0

--- a/solution.py
+++ b/solution.py
@@ -6,6 +6,11 @@
 
 EPSILON = 1e-06
 KEPT_SHARE = 1.0 / 64
+
+
+def gather_from_all(x, axis, dim):
+    copies = jnp.concatenate([x] * lax.axis_size(axis), axis=dim)
+    return lax.all_to_all(copies, axis, dim, dim, tiled=True)
 
 
 def neighbours(rows, axis):
@@ -52,7 +57,7 @@
         held = jnp.where(
             upper, jnp.concatenate([got, held], axis=0), jnp.concatenate([held, got], axis=0)
         )
-    return lax.all_gather(held.reshape(-1, block.shape[-1]), "gy", axis=0, tiled=True)
+    return gather_from_all(held.reshape(-1, block.shape[-1]), "gy", 0)
 
 
 def gathered_order(rounds, count_y):

time: 484 us -> 508 us (1.050)
  the two profiles are of different devices: /device:TPU:8 before, /device:TPU:384 now
where the time goes in v1:
time: 508 us; the launch traced here: 506 us
  waiting for transfers between devices  243 us (48%)
  starting transfers between devices  145 us (29%)
  local copies, waits for them, and re-layouts  44 us (9%)
  blocking collectives  39.4 us (8%)
  matrix products  22.4 us (4%)
  other arithmetic  8.34 us (2%)
    ppermute x18, waiting for transfers between devices, allsum(): lax.ppermute(value, axis, [(i, i ^ step) for i in range(count)])  91.6 us
    ppermute x12, waiting for transfers between devices, doubling_gather(): got = lax.ppermute(held, axis, [(i, i ^ step) for i in range(count)])  68.5 us
    all_to_all x2, waiting for transfers between devices, gather_from_all(): return lax.all_to_all(copies, axis, dim, dim, tiled=True)  61 us
    ppermute x18, starting transfers between devices, allsum(): lax.ppermute(value, axis, [(i, i ^ step) for i in range(count)])  51.8 us
    ppermute x16, starting transfers between devices, neighbours(): return (lax.ppermute(rows[1], axis, up), lax.ppermute(rows[0], axis, down))  46 us
    psum x3, blocking collectives, allsum(): value = lax.psum(value, 'gy')  39.4 us
    ppermute x12, starting transfers between devices, doubling_gather(): got = lax.ppermute(held, axis, [(i, i ^ step) for i in range(count)])  38.3 us
    ppermute x16, waiting for transfers between devices, neighbours(): return (lax.ppermute(rows[1], axis, up), lax.ppermute(rows[0], axis, down))  22.3 us
  transfers between devices with their start and end apart: 48, of which 37 were waited for; matrix products, arithmetic and copies ran while one was open for 1% of the time, Pallas kernels for 0%

profile of v1, /device:TPU:384, one launch (start us, length us, event | category | flops | bytes accessed | tf_op | source)
XLA Modules:
  0.0 506.0 jit_solution(656187828637317244)
XLA Ops:
  1.6 14.6 %psum.35 = f32[128]{0:T(128)S(1)} all-reduce(f32[128]{0:T(128)S(1)} %multiply_reduce_fusion.10), channel_id=1, replica_groups=mesh['gx'=64,'gy'=8] {'gy'}, use_global_device_ids=true, to_apply=%region_1.0 | all-reduce | flops 128 | bytes 1024 | tf_op jit(solution)/shard_map/psum | solution.py:30
  21.7 5.1 %collective-permute-start.13 = (f32[128]{0:T(128)S(1)}, f32[128]{0:T(128)S(1)}, u32[]{:S(2)}, u32[]{:S(2)}) collective-permute-start(f32[128]{0:T(128)S(1)} %add.219), channel_id=1, source_target_pairs={{0,16},{8,24},{16,0},{24,8},{32,48},{40,56},{48,32},{56,40},{64,80... | collective-permute-start | bytes 1544 | tf_op jit(solution)/shard_map/ppermute | solution.py:38
  40.4 5.4 %collective-permute-start.16 = (f32[128]{0:T(128)S(1)}, f32[128]{0:T(128)S(1)}, u32[]{:S(2)}, u32[]{:S(2)}) collective-permute-start(f32[128]{0:T(128)S(1)} %add.222), channel_id=1, source_target_pairs={{0,128},{8,136},{16,144},{24,152},{32,160},{40,168},{48,176},{56,1... | collective-permute-start | bytes 1544 | tf_op jit(solution)/shard_map/ppermute | solution.py:38
  53.8 10.2 %collective-permute-done.17 = f32[128]{0:T(128)S(1)} collective-permute-done((f32[128]{0:T(128)S(1)}, f32[128]{0:T(128)S(1)}, u32[]{:S(2)}, u32[]{:S(2)}) %collective-permute-start.17) | collective-permute-done | bytes 544 | tf_op jit(solution)/shard_map/ppermute | solution.py:38
  69.0 10.2 %collective-permute-done.22 = bf16[1,32,128]{2,1,0:T(8,128)(2,1)S(1)} collective-permute-done((bf16[1,32,128]{2,1,0:T(8,128)(2,1)S(1)}, bf16[1,32,128]{2,1,0:T(8,128)(2,1)S(1)}, u32[]{:S(2)}, u32[]{:S(2)}) %collective-permute-start.22) | collective-permute-done | bytes 8224 | tf_op jit(solution)/shard_map/ppermute | solution.py:55
  79.2 5.4 %collective-permute-start.23 = (bf16[2,32,128]{2,1,0:T(8,128)(2,1)S(1)}, bf16[2,32,128]{2,1,0:T(8,128)(2,1)S(1)}, u32[]{:S(2)}, u32[]{:S(2)}) collective-permute-start(bf16[2,32,128]{2,1,0:T(8,128)(2,1)S(1)} %maximum_select_fusion.10), channel_id=1, source_target_pairs={{0,128},{8,136},{16,144},{24,152},{32,160},{40,168},{48,176},{56,1... | collective-permute-start | bytes 49160 | tf_op jit(solution)/shard_map/ppermute | solution.py:55
  101.7 5.1 %collective-permute-start.26 = (bf16[16,32,128]{2,1,0:T(8,128)(2,1)S(1)}, bf16[16,32,128]{2,1,0:T(8,128)(2,1)S(1)}, u32[]{:S(2)}, u32[]{:S(2)}) collective-permute-start(bf16[16,32,128]{2,1,0:T(8,128)(2,1)S(1)} %maximum_select_fusion.4), channel_id=1, source_target_pairs={{0,16},{8,24},{16,0},{24,8},{32,48},{40,56},{48,32},{56,40},{64,80... | collective-permute-start | bytes 393224 | tf_op jit(solution)/shard_map/ppermute | solution.py:55
  131.2 6.6 %collective-permute-start.19 = (f32[128,128]{1,0:T(8,128)S(1)}, f32[128,128]{1,0:T(8,128)S(1)}, u32[]{:S(2)}, u32[]{:S(2)}) collective-permute-start(f32[128,128]{1,0:T(8,128)S(1)} %get-tuple-element.66), channel_id=1, source_target_pairs={{8,0},{16,8},{24,16},{32,24},{40,32},{48,40},{56,48},{64,56},{72,6... | collective-permute-start | bytes 196616 | tf_op jit(solution)/shard_map/ppermute | solution.py:20
  148.0 28.0 %all-to-all-done = bf16[8,2048,128]{2,1,0:T(8,128)(2,1)} async-done(((bf16[8,2048,128]{2,1,0:T(8,128)(2,1)}), bf16[8,2048,128]{2,1,0:T(8,128)(2,1)}, u32[]{:S(2)}, u32[]{:S(2)}) %all-to-all-start) | async-done | bytes 4194336 | tf_op jit(solution)/shard_map/all_to_all | solution.py:13
  175.9 7.4 %reshape.138 = bf16[512,4096]{1,0:T(8,128)(2,1)} reshape(bf16[8,2048,128]{2,1,0:T(8,128)(2,1)} %all-to-all-done) | data formatting | bytes 8388608 | tf_op jit(solution)/shard_map/reshape | solution.py:129
  183.3 6.6 %convolution_convert_fusion.1 = bf16[512,4096]{1,0:T(8,128)(2,1)} fusion(bf16[512,4096]{1,0:T(8,128)(2,1)} %reshape.138, s32[512]{0:T(512)S(1)} %gather_fusion.1), kind=kOutput, calls=%fused_computation.10 | convolution fusion | flops 2149842944 | bytes 8390656 | tf_op jit(solution)/shard_map/dot_general | solution.py:130
  189.9 7.5 %reshape.139 = bf16[16384,128]{1,0:T(8,128)(2,1)} reshape(bf16[512,4096]{1,0:T(8,128)(2,1)} %convolution_convert_fusion.1) | data formatting | bytes 8388608 | tf_op jit(solution)/shard_map/reshape | solution.py:134
  206.8 6.6 %collective-permute-start.29 = (bf16[128,128]{1,0:T(8,128)(2,1)S(1)}, bf16[128,128]{1,0:T(8,128)(2,1)S(1)}, u32[]{:S(2)}, u32[]{:S(2)}) collective-permute-start(bf16[128,128]{1,0:T(8,128)(2,1)S(1)} %get-tuple-element.74), channel_id=1, source_target_pairs={{8,0},{16,8},{24,16},{32,24},{40,32},{48,40},{56,48},{64,56},{72,6... | collective-permute-start | bytes 98312 | tf_op jit(solution)/shard_map/ppermute | solution.py:20
  215.4 7.2 %collective-permute-done.28 = bf16[128,128]{1,0:T(8,128)(2,1)S(1)} collective-permute-done((bf16[128,128]{1,0:T(8,128)(2,1)S(1)}, bf16[128,128]{1,0:T(8,128)(2,1)S(1)}, u32[]{:S(2)}, u32[]{:S(2)}) %collective-permute-start.28) | collective-permute-done | bytes 32800 | tf_op jit(solution)/shard_map/ppermute | solution.py:20
  225.2 12.4 %psum.36 = f32[3,128]{1,0:T(4,128)S(1)} all-reduce(f32[3,128]{1,0:T(4,128)S(1)} %pad_maximum_fusion.4), channel_id=1, replica_groups=mesh['gx'=64,'gy'=8] {'gy'}, use_global_device_ids=true, to_apply=%region_6.7 | all-reduce | flops 384 | bytes 3072 | tf_op jit(solution)/shard_map/psum | solution.py:30
  245.0 5.1 collective-permute-done.33
  265.6 5.7 %collective-permute-done.36 = f32[3,128]{1,0:T(4,128)S(1)} collective-permute-done((f32[3,128]{1,0:T(4,128)S(1)}, f32[3,128]{1,0:T(4,128)S(1)}, u32[]{:S(2)}, u32[]{:S(2)}) %collective-permute-start.36) | collective-permute-done | bytes 1568 | tf_op jit(solution)/shard_map/ppermute | solution.py:38
  274.1 11.4 %collective-permute-done.37 = f32[3,128]{1,0:T(4,128)S(1)} collective-permute-done((f32[3,128]{1,0:T(4,128)S(1)}, f32[3,128]{1,0:T(4,128)S(1)}, u32[]{:S(2)}, u32[]{:S(2)}) %collective-permute-start.37) | collective-permute-done | bytes 1568 | tf_op jit(solution)/shard_map/ppermute | solution.py:38
  289.8 11.8 %collective-permute-done.42 = bf16[1,32,128]{2,1,0:T(8,128)(2,1)S(1)} collective-permute-done((bf16[1,32,128]{2,1,0:T(8,128)(2,1)S(1)}, bf16[1,32,128]{2,1,0:T(8,128)(2,1)S(1)}, u32[]{:S(2)}, u32[]{:S(2)}) %collective-permute-start.42) | collective-permute-done | bytes 8224 | tf_op jit(solution)/shard_map/ppermute | solution.py:55
  304.9 6.4 %collective-permute-done.43 = bf16[2,32,128]{2,1,0:T(8,128)(2,1)S(1)} collective-permute-done((bf16[2,32,128]{2,1,0:T(8,128)(2,1)S(1)}, bf16[2,32,128]{2,1,0:T(8,128)(2,1)S(1)}, u32[]{:S(2)}, u32[]{:S(2)}) %collective-permute-start.43) | collective-permute-done | bytes 16416 | tf_op jit(solution)/shard_map/ppermute | solution.py:55
  326.1 6.4 %collective-permute-done.46 = bf16[16,32,128]{2,1,0:T(8,128)(2,1)S(1)} collective-permute-done((bf16[16,32,128]{2,1,0:T(8,128)(2,1)S(1)}, bf16[16,32,128]{2,1,0:T(8,128)(2,1)S(1)}, u32[]{:S(2)}, u32[]{:S(2)}) %collective-permute-start.46) | collective-permute-done | bytes 131104 | tf_op jit(solution)/shard_map/ppermute | solution.py:55
  334.7 6.2 %collective-permute-done.47 = bf16[32,32,128]{2,1,0:T(8,128)(2,1)S(1)} collective-permute-done((bf16[32,32,128]{2,1,0:T(8,128)(2,1)S(1)}, bf16[32,32,128]{2,1,0:T(8,128)(2,1)S(1)}, u32[]{:S(2)}, u32[]{:S(2)}) %collective-permute-start.47) | collective-permute-done | bytes 262176 | tf_op jit(solution)/shard_map/ppermute | solution.py:55
  359.7 5.2 %collective-permute-done.38 = f32[128,128]{1,0:T(8,128)S(1)} collective-permute-done((f32[128,128]{1,0:T(8,128)S(1)}, f32[128,128]{1,0:T(8,128)S(1)}, u32[]{:S(2)}, u32[]{:S(2)}) %collective-permute-start.38) | collective-permute-done | bytes 65568 | tf_op jit(solution)/shard_map/ppermute | solution.py:20
  365.3 33.0 %all-to-all-done.1 = bf16[8,2048,128]{2,1,0:T(8,128)(2,1)} async-done(((bf16[8,2048,128]{2,1,0:T(8,128)(2,1)}), bf16[8,2048,128]{2,1,0:T(8,128)(2,1)}, u32[]{:S(2)}, u32[]{:S(2)}) %all-to-all-start.1) | async-done | bytes 4194336 | tf_op jit(solution)/shard_map/all_to_all | solution.py:13
  398.3 7.4 %reshape.141 = bf16[512,4096]{1,0:T(8,128)(2,1)} reshape(bf16[8,2048,128]{2,1,0:T(8,128)(2,1)} %all-to-all-done.1) | data formatting | bytes 8388608 | tf_op jit(solution)/shard_map/reshape | solution.py:129
  405.7 6.6 %convolution_convert_fusion = bf16[512,4096]{1,0:T(8,128)(2,1)} fusion(bf16[512,4096]{1,0:T(8,128)(2,1)} %reshape.141, s32[512]{0:T(512)S(1)} %gather_fusion.1), kind=kOutput, calls=%fused_computation.9 | convolution fusion | flops 2149842944 | bytes 8390656 | tf_op jit(solution)/shard_map/dot_general | solution.py:130
  412.3 7.4 %reshape.142 = bf16[16384,128]{1,0:T(8,128)(2,1)} reshape(bf16[512,4096]{1,0:T(8,128)(2,1)} %convolution_convert_fusion) | data formatting | bytes 8388608 | tf_op jit(solution)/shard_map/reshape | solution.py:134
  435.0 5.2 %collective-permute-done.48 = bf16[128,128]{1,0:T(8,128)(2,1)S(1)} collective-permute-done((bf16[128,128]{1,0:T(8,128)(2,1)S(1)}, bf16[128,128]{1,0:T(8,128)(2,1)S(1)}, u32[]{:S(2)}, u32[]{:S(2)}) %collective-permute-start.48) | collective-permute-done | bytes 32800 | tf_op jit(solution)/shard_map/ppermute | solution.py:20
  442.8 12.4 %psum.37 = f32[6,128]{1,0:T(8,128)S(1)} all-reduce(f32[6,128]{1,0:T(8,128)S(1)} %stack.126), channel_id=1, replica_groups=mesh['gx'=64,'gy'=8] {'gy'}, use_global_device_ids=true, to_apply=%region_18.19 | all-reduce | flops 768 | bytes 6144 | tf_op jit(solution)/shard_map/psum | solution.py:30
  462.7 5.1 %collective-permute-done.53 = f32[6,128]{1,0:T(8,128)S(1)} collective-permute-done((f32[6,128]{1,0:T(8,128)S(1)}, f32[6,128]{1,0:T(8,128)S(1)}, u32[]{:S(2)}, u32[]{:S(2)}) %collective-permute-start.53) | collective-permute-done | bytes 3104 | tf_op jit(solution)/shard_map/ppermute | solution.py:38
  483.1 5.9 %collective-permute-done.56 = f32[6,128]{1,0:T(8,128)S(1)} collective-permute-done((f32[6,128]{1,0:T(8,128)S(1)}, f32[6,128]{1,0:T(8,128)S(1)}, u32[]{:S(2)}, u32[]{:S(2)}) %collective-permute-start.56) | collective-permute-done | bytes 3104 | tf_op jit(solution)/shard_map/ppermute | solution.py:38
  491.4 11.8 %collective-permute-done.57 = f32[6,128]{1,0:T(8,128)S(1)} collective-permute-done((f32[6,128]{1,0:T(8,128)S(1)}, f32[6,128]{1,0:T(8,128)S(1)}, u32[]{:S(2)}, u32[]{:S(2)}) %collective-permute-start.57) | collective-permute-done | bytes 3104 | tf_op jit(solution)/shard_map/ppermute | solution.py:38
  (191 shorter events, 211.7 us)
Async XLA Ops:
  40.4 9.4 %collective-permute-start.16 = (f32[128]{0:T(128)S(1)}, f32[128]{0:T(128)S(1)}, u32[]{:S(2)}, u32[]{:S(2)}) collective-permute-start(f32[128]{0:T(128)S(1)} %add.222), channel_id=1, source_target_pairs={{0,128},{8,136},{16,144},{24,152},{32,160},{40,168},{48,176},{56,1... | collective-permute-start | bytes 1544 | tf_op jit(solution)/shard_map/ppermute | solution.py:38
  49.8 14.2 %collective-permute-start.17 = (f32[128]{0:T(128)S(1)}, f32[128]{0:T(128)S(1)}, u32[]{:S(2)}, u32[]{:S(2)}) collective-permute-start(f32[128]{0:T(128)S(1)} %add.223), channel_id=1, source_target_pairs={{0,256},{8,264},{16,272},{24,280},{32,288},{40,296},{48,304},{56,3... | collective-permute-start | bytes 1544 | tf_op jit(solution)/shard_map/ppermute | solution.py:38
  65.0 14.3 %collective-permute-start.22 = (bf16[1,32,128]{2,1,0:T(8,128)(2,1)S(1)}, bf16[1,32,128]{2,1,0:T(8,128)(2,1)S(1)}, u32[]{:S(2)}, u32[]{:S(2)}) collective-permute-start(bf16[1,32,128]{2,1,0:T(8,128)(2,1)S(1)} %fusion.2), channel_id=1, source_target_pairs={{0,256},{8,264},{16,272},{24,280},{32,288},{40,296},{48,304},{56,3... | collective-permute-start | bytes 24584 | tf_op jit(solution)/shard_map/ppermute | solution.py:55
  79.2 9.5 %collective-permute-start.23 = (bf16[2,32,128]{2,1,0:T(8,128)(2,1)S(1)}, bf16[2,32,128]{2,1,0:T(8,128)(2,1)S(1)}, u32[]{:S(2)}, u32[]{:S(2)}) collective-permute-start(bf16[2,32,128]{2,1,0:T(8,128)(2,1)S(1)} %maximum_select_fusion.10), channel_id=1, source_target_pairs={{0,128},{8,136},{16,144},{24,152},{32,160},{40,168},{48,176},{56,1... | collective-permute-start | bytes 49160 | tf_op jit(solution)/shard_map/ppermute | solution.py:55
  101.7 8.4 %collective-permute-start.26 = (bf16[16,32,128]{2,1,0:T(8,128)(2,1)S(1)}, bf16[16,32,128]{2,1,0:T(8,128)(2,1)S(1)}, u32[]{:S(2)}, u32[]{:S(2)}) collective-permute-start(bf16[16,32,128]{2,1,0:T(8,128)(2,1)S(1)} %maximum_select_fusion.4), channel_id=1, source_target_pairs={{0,16},{8,24},{16,0},{24,8},{32,48},{40,56},{48,32},{56,40},{64,80... | collective-permute-start | bytes 393224 | tf_op jit(solution)/shard_map/ppermute | solution.py:55
  110.0 8.3 %collective-permute-start.27 = (bf16[32,32,128]{2,1,0:T(8,128)(2,1)S(1)}, bf16[32,32,128]{2,1,0:T(8,128)(2,1)S(1)}, u32[]{:S(2)}, u32[]{:S(2)}) collective-permute-start(bf16[32,32,128]{2,1,0:T(8,128)(2,1)S(1)} %maximum_select_fusion.2), channel_id=1, source_target_pairs={{0,8},{8,0},{16,24},{24,16},{32,40},{40,32},{48,56},{56,48},{64,72... | collective-permute-start | bytes 786440 | tf_op jit(solution)/shard_map/ppermute | solution.py:55
  121.0 54.9 %all-to-all-start = ((bf16[8,2048,128]{2,1,0:T(8,128)(2,1)}), bf16[8,2048,128]{2,1,0:T(8,128)(2,1)}, u32[]{:S(2)}, u32[]{:S(2)}) async-start(bf16[8,2048,128]{2,1,0:T(8,128)(2,1)} %bitcast.207), calls=%async_computation | async-start | bytes 8388608 | tf_op jit(solution)/shard_map/all_to_all | solution.py:13
  126.9 16.4 %collective-permute-start.21 = (f32[128,128]{1,0:T(8,128)S(1)}, f32[128,128]{1,0:T(8,128)S(1)}, u32[]{:S(2)}, u32[]{:S(2)}) collective-permute-start(f32[128,128]{1,0:T(8,128)S(1)} %get-tuple-element.67), channel_id=1, source_target_pairs={{1,0},{2,1},{3,2},{4,3},{5,4},{6,5},{7,6},{9,8},{10,9},{11,10},{12... | collective-permute-start | bytes 196616 | tf_op jit(solution)/shard_map/ppermute | solution.py:20
  128.2 15.1 %collective-permute-start.20 = (f32[128,128]{1,0:T(8,128)S(1)}, f32[128,128]{1,0:T(8,128)S(1)}, u32[]{:S(2)}, u32[]{:S(2)}) collective-permute-start(f32[128,128]{1,0:T(8,128)S(1)} %get-tuple-element.65), channel_id=1, source_target_pairs={{0,1},{1,2},{2,3},{3,4},{4,5},{5,6},{6,7},{8,9},{9,10},{10,11},{11... | collective-permute-start | bytes 196616 | tf_op jit(solution)/shard_map/ppermute | solution.py:20
  131.2 12.1 %collective-permute-start.19 = (f32[128,128]{1,0:T(8,128)S(1)}, f32[128,128]{1,0:T(8,128)S(1)}, u32[]{:S(2)}, u32[]{:S(2)}) collective-permute-start(f32[128,128]{1,0:T(8,128)S(1)} %get-tuple-element.66), channel_id=1, source_target_pairs={{8,0},{16,8},{24,16},{32,24},{40,32},{48,40},{56,48},{64,56},{72,6... | collective-permute-start | bytes 196616 | tf_op jit(solution)/shard_map/ppermute | solution.py:20
  137.8 9.8 %collective-permute-start.18 = (f32[128,128]{1,0:T(8,128)S(1)}, f32[128,128]{1,0:T(8,128)S(1)}, u32[]{:S(2)}, u32[]{:S(2)}) collective-permute-start(f32[128,128]{1,0:T(8,128)S(1)} %get-tuple-element.64), channel_id=1, source_target_pairs={{0,8},{8,16},{16,24},{24,32},{32,40},{40,48},{48,56},{56,64},{64,7... | collective-permute-start | bytes 196616 | tf_op jit(solution)/shard_map/ppermute | solution.py:20
  202.5 12.9 %collective-permute-start.31 = (bf16[128,128]{1,0:T(8,128)(2,1)S(1)}, bf16[128,128]{1,0:T(8,128)(2,1)S(1)}, u32[]{:S(2)}, u32[]{:S(2)}) collective-permute-start(bf16[128,128]{1,0:T(8,128)(2,1)S(1)} %get-tuple-element.75), channel_id=1, source_target_pairs={{1,0},{2,1},{3,2},{4,3},{5,4},{6,5},{7,6},{9,8},{10,9},{11,10},{12... | collective-permute-start | bytes 98312 | tf_op jit(solution)/shard_map/ppermute | solution.py:20
  203.8 11.6 %collective-permute-start.30 = (bf16[128,128]{1,0:T(8,128)(2,1)S(1)}, bf16[128,128]{1,0:T(8,128)(2,1)S(1)}, u32[]{:S(2)}, u32[]{:S(2)}) collective-permute-start(bf16[128,128]{1,0:T(8,128)(2,1)S(1)} %get-tuple-element.73), channel_id=1, source_target_pairs={{0,1},{1,2},{2,3},{3,4},{4,5},{5,6},{6,7},{8,9},{9,10},{10,11},{11... | collective-permute-start | bytes 98312 | tf_op jit(solution)/shard_map/ppermute | solution.py:20
  206.8 8.6 %collective-permute-start.29 = (bf16[128,128]{1,0:T(8,128)(2,1)S(1)}, bf16[128,128]{1,0:T(8,128)(2,1)S(1)}, u32[]{:S(2)}, u32[]{:S(2)}) collective-permute-start(bf16[128,128]{1,0:T(8,128)(2,1)S(1)} %get-tuple-element.74), channel_id=1, source_target_pairs={{8,0},{16,8},{24,16},{32,24},{40,32},{48,40},{56,48},{64,56},{72,6... | collective-permute-start | bytes 98312 | tf_op jit(solution)/shard_map/ppermute | solution.py:20
  213.4 9.1 %collective-permute-start.28 = (bf16[128,128]{1,0:T(8,128)(2,1)S(1)}, bf16[128,128]{1,0:T(8,128)(2,1)S(1)}, u32[]{:S(2)}, u32[]{:S(2)}) collective-permute-start(bf16[128,128]{1,0:T(8,128)(2,1)S(1)} %get-tuple-element.72), channel_id=1, source_target_pairs={{0,8},{8,16},{16,24},{24,32},{32,40},{40,48},{48,56},{56,64},{64,7... | collective-permute-start | bytes 98312 | tf_op jit(solution)/shard_map/ppermute | solution.py:20
  243.1 7.0 %collective-permute-start.33 = (f32[3,128]{1,0:T(4,128)S(1)}, f32[3,128]{1,0:T(4,128)S(1)}, u32[]{:S(2)}, u32[]{:S(2)}) collective-permute-start(f32[3,128]{1,0:T(4,128)S(1)} %add.237), channel_id=1, source_target_pairs={{0,16},{8,24},{16,0},{24,8},{32,48},{40,56},{48,32},{56,40},{64,80... | collective-permute-start | bytes 4616 | tf_op jit(solution)/shard_map/ppermute | solution.py:38
  261.9 9.4 %collective-permute-start.36 = (f32[3,128]{1,0:T(4,128)S(1)}, f32[3,128]{1,0:T(4,128)S(1)}, u32[]{:S(2)}, u32[]{:S(2)}) collective-permute-start(f32[3,128]{1,0:T(4,128)S(1)} %add.240), channel_id=1, source_target_pairs={{0,128},{8,136},{16,144},{24,152},{32,160},{40,168},{48,176},{56,1... | collective-permute-start | bytes 4616 | tf_op jit(solution)/shard_map/ppermute | solution.py:38
  271.3 14.2 %collective-permute-start.37 = (f32[3,128]{1,0:T(4,128)S(1)}, f32[3,128]{1,0:T(4,128)S(1)}, u32[]{:S(2)}, u32[]{:S(2)}) collective-permute-start(f32[3,128]{1,0:T(4,128)S(1)} %add.241), channel_id=1, source_target_pairs={{0,256},{8,264},{16,272},{24,280},{32,288},{40,296},{48,304},{56,3... | collective-permute-start | bytes 4616 | tf_op jit(solution)/shard_map/ppermute | solution.py:38
  287.0 14.6 %collective-permute-start.42 = (bf16[1,32,128]{2,1,0:T(8,128)(2,1)S(1)}, bf16[1,32,128]{2,1,0:T(8,128)(2,1)S(1)}, u32[]{:S(2)}, u32[]{:S(2)}) collective-permute-start(bf16[1,32,128]{2,1,0:T(8,128)(2,1)S(1)} %fusion.3), channel_id=1, source_target_pairs={{0,256},{8,264},{16,272},{24,280},{32,288},{40,296},{48,304},{56,3... | collective-permute-start | bytes 24584 | tf_op jit(solution)/shard_map/ppermute | solution.py:55
  301.6 9.6 %collective-permute-start.43 = (bf16[2,32,128]{2,1,0:T(8,128)(2,1)S(1)}, bf16[2,32,128]{2,1,0:T(8,128)(2,1)S(1)}, u32[]{:S(2)}, u32[]{:S(2)}) collective-permute-start(bf16[2,32,128]{2,1,0:T(8,128)(2,1)S(1)} %maximum_select_fusion.11), channel_id=1, source_target_pairs={{0,128},{8,136},{16,144},{24,152},{32,160},{40,168},{48,176},{56,1... | collective-permute-start | bytes 49160 | tf_op jit(solution)/shard_map/ppermute | solution.py:55
  324.2 8.4 %collective-permute-start.46 = (bf16[16,32,128]{2,1,0:T(8,128)(2,1)S(1)}, bf16[16,32,128]{2,1,0:T(8,128)(2,1)S(1)}, u32[]{:S(2)}, u32[]{:S(2)}) collective-permute-start(bf16[16,32,128]{2,1,0:T(8,128)(2,1)S(1)} %maximum_select_fusion.5), channel_id=1, source_target_pairs={{0,16},{8,24},{16,0},{24,8},{32,48},{40,56},{48,32},{56,40},{64,80... | collective-permute-start | bytes 393224 | tf_op jit(solution)/shard_map/ppermute | solution.py:55
  332.6 8.3 %collective-permute-start.47 = (bf16[32,32,128]{2,1,0:T(8,128)(2,1)S(1)}, bf16[32,32,128]{2,1,0:T(8,128)(2,1)S(1)}, u32[]{:S(2)}, u32[]{:S(2)}) collective-permute-start(bf16[32,32,128]{2,1,0:T(8,128)(2,1)S(1)} %maximum_select_fusion.3), channel_id=1, source_target_pairs={{0,8},{8,0},{16,24},{24,16},{32,40},{40,32},{48,56},{56,48},{64,72... | collective-permute-start | bytes 786440 | tf_op jit(solution)/shard_map/ppermute | solution.py:55
  343.5 54.8 %all-to-all-start.1 = ((bf16[8,2048,128]{2,1,0:T(8,128)(2,1)}), bf16[8,2048,128]{2,1,0:T(8,128)(2,1)}, u32[]{:S(2)}, u32[]{:S(2)}) async-start(bf16[8,2048,128]{2,1,0:T(8,128)(2,1)} %bitcast.208), calls=%async_computation.1 | async-start | bytes 8388608 | tf_op jit(solution)/shard_map/all_to_all | solution.py:13
  349.2 10.2 %collective-permute-start.41 = (f32[128,128]{1,0:T(8,128)S(1)}, f32[128,128]{1,0:T(8,128)S(1)}, u32[]{:S(2)}, u32[]{:S(2)}) collective-permute-start(f32[128,128]{1,0:T(8,128)S(1)} %get-tuple-element.63), channel_id=1, source_target_pairs={{1,0},{2,1},{3,2},{4,3},{5,4},{6,5},{7,6},{9,8},{10,9},{11,10},{12... | collective-permute-start | bytes 196616 | tf_op jit(solution)/shard_map/ppermute | solution.py:20
  350.5 8.9 %collective-permute-start.40 = (f32[128,128]{1,0:T(8,128)S(1)}, f32[128,128]{1,0:T(8,128)S(1)}, u32[]{:S(2)}, u32[]{:S(2)}) collective-permute-start(f32[128,128]{1,0:T(8,128)S(1)} %get-tuple-element.61), channel_id=1, source_target_pairs={{0,1},{1,2},{2,3},{3,4},{4,5},{5,6},{6,7},{8,9},{9,10},{10,11},{11... | collective-permute-start | bytes 196616 | tf_op jit(solution)/shard_map/ppermute | solution.py:20
  355.4 9.5 %collective-permute-start.38 = (f32[128,128]{1,0:T(8,128)S(1)}, f32[128,128]{1,0:T(8,128)S(1)}, u32[]{:S(2)}, u32[]{:S(2)}) collective-permute-start(f32[128,128]{1,0:T(8,128)S(1)} %get-tuple-element.60), channel_id=1, source_target_pairs={{0,8},{8,16},{16,24},{24,32},{32,40},{40,48},{48,56},{56,64},{64,7... | collective-permute-start | bytes 196616 | tf_op jit(solution)/shard_map/ppermute | solution.py:20
  424.8 10.2 %collective-permute-start.51 = (bf16[128,128]{1,0:T(8,128)(2,1)S(1)}, bf16[128,128]{1,0:T(8,128)(2,1)S(1)}, u32[]{:S(2)}, u32[]{:S(2)}) collective-permute-start(bf16[128,128]{1,0:T(8,128)(2,1)S(1)} %get-tuple-element.71), channel_id=1, source_target_pairs={{1,0},{2,1},{3,2},{4,3},{5,4},{6,5},{7,6},{9,8},{10,9},{11,10},{12... | collective-permute-start | bytes 98312 | tf_op jit(solution)/shard_map/ppermute | solution.py:20
  426.1 8.9 %collective-permute-start.50 = (bf16[128,128]{1,0:T(8,128)(2,1)S(1)}, bf16[128,128]{1,0:T(8,128)(2,1)S(1)}, u32[]{:S(2)}, u32[]{:S(2)}) collective-permute-start(bf16[128,128]{1,0:T(8,128)(2,1)S(1)} %get-tuple-element.69), channel_id=1, source_target_pairs={{0,1},{1,2},{2,3},{3,4},{4,5},{5,6},{6,7},{8,9},{9,10},{10,11},{11... | collective-permute-start | bytes 98312 | tf_op jit(solution)/shard_map/ppermute | solution.py:20
  431.1 9.1 %collective-permute-start.48 = (bf16[128,128]{1,0:T(8,128)(2,1)S(1)}, bf16[128,128]{1,0:T(8,128)(2,1)S(1)}, u32[]{:S(2)}, u32[]{:S(2)}) collective-permute-start(bf16[128,128]{1,0:T(8,128)(2,1)S(1)} %get-tuple-element.68), channel_id=1, source_target_pairs={{0,8},{8,16},{16,24},{24,32},{32,40},{40,48},{48,56},{56,64},{64,7... | collective-permute-start | bytes 98312 | tf_op jit(solution)/shard_map/ppermute | solution.py:20
  460.8 7.0 %collective-permute-start.53 = (f32[6,128]{1,0:T(8,128)S(1)}, f32[6,128]{1,0:T(8,128)S(1)}, u32[]{:S(2)}, u32[]{:S(2)}) collective-permute-start(f32[6,128]{1,0:T(8,128)S(1)} %add.247), channel_id=1, source_target_pairs={{0,16},{8,24},{16,0},{24,8},{32,48},{40,56},{48,32},{56,40},{64,80... | collective-permute-start | bytes 9224 | tf_op jit(solution)/shard_map/ppermute | solution.py:38
  479.6 9.4 %collective-permute-start.56 = (f32[6,128]{1,0:T(8,128)S(1)}, f32[6,128]{1,0:T(8,128)S(1)}, u32[]{:S(2)}, u32[]{:S(2)}) collective-permute-start(f32[6,128]{1,0:T(8,128)S(1)} %add.250), channel_id=1, source_target_pairs={{0,128},{8,136},{16,144},{24,152},{32,160},{40,168},{48,176},{56,1... | collective-permute-start | bytes 9224 | tf_op jit(solution)/shard_map/ppermute | solution.py:38
  489.0 14.2 %collective-permute-start.57 = (f32[6,128]{1,0:T(8,128)S(1)}, f32[6,128]{1,0:T(8,128)S(1)}, u32[]{:S(2)}, u32[]{:S(2)}) collective-permute-start(f32[6,128]{1,0:T(8,128)S(1)} %add.251), channel_id=1, source_target_pairs={{0,256},{8,264},{16,272},{24,280},{32,288},{40,296},{48,304},{56,3... | collective-permute-start | bytes 9224 | tf_op jit(solution)/shard_map/ppermute | solution.py:38
  (27 other events, 426.7 us)
